TPU v7x, 32 devices: a whole 2x2x4 slice. The times are simulated.
32 devices in a mesh: req: 8 (over z, y), tp: 4 (over x, core).
Axes of the slice: x: 2, y: 2, z: 4, core: 2. Of those that a mesh axis runs over, the one named last changes fastest.
Arguments:
- hidden_in: bfloat16 [192, 1536], P('req', 'tp'), may hold values from -12 to 12
- queries: bfloat16 [192, 1536], P('req', 'tp'), may hold values from -6 to 6
- fresh_key_value: bfloat16 [192, 2, 256], P('req'), may hold values from -120 to 120
- positions: int32 [192], P('req'), may hold values from 0 to 4095
- lengths: int32 [8, 24], P('req'), may hold values from 1 to 2048, 3072 in all within a row
- cache: bfloat16 [24576, 2, 2, 128], P(('req', 'tp')), may hold values from -160 to 160
- out_proj: bfloat16 [1536, 1536], P('tp'), may hold values from -0.59765625 to 0.59765625
- norm_gain: float32 [1536], replicated, may hold values from 0.1 to 1.9
- expert_ids: int32 [192, 4], P('req'), may hold values from 0 to 31, all different within a row; in each aligned block of 24 rows (0 to 23, 24 to 47, ...) at most 8 rows name the same one
- router_weights: float32 [192, 4], P('req'), may hold values from 0.05 to 0.5
- gate_up: bfloat16 [32, 2, 1536, 768], P('req', None, None, 'tp'), may hold values from -0.15625 to 0.15625
- down: bfloat16 [32, 768, 1536], P('req', 'tp'), may hold values from -0.21875 to 0.21875
Outputs:
- layer_out: bfloat16 [192, 1536], P('req', 'tp')
Inputs may be any that keep to these rules, and one draw needn't show every extreme that they name: `lengths`: each row sums to 3072. `expert_ids`: each row names 4 different experts; among the 24 aligned rows of one request group no expert is named by more than 8 rows, a bound that some block reaches.
All inputs are finite; a program needn't handle non-finite values.
Results may differ from a plain program's by a relative error of at most 0.012.
The roundings to bfloat16 on the way count: a program that leaves them out, or rounds other values in their place, can miss the bound.
Values may be sent and summed in bfloat16 or wider, within the bound.
No kernel may reach another device: no remote copies, remote signals or barrier semaphores. Data moves between devices by JAX's collectives and lax.ppermute only.
A program may use at most 64 MiB of HBM per device.

v0:
```python
import jax
import jax.numpy as jnp
from jax import lax
from jax.sharding import PartitionSpec as P

EXPERTS = 32
rope_base = 1000000.0
norm_eps = 1e-06
neg_floor = -1e30


def apply_rotary_heads(values, positions, head_size):
    half_size = head_size // 2
    exponents = jnp.arange(half_size, dtype=jnp.float32) * (2.0 / head_size)
    inverse_freq = jnp.power(jnp.float32(rope_base), -exponents)
    angles = positions.astype(jnp.float32)[:, None] * inverse_freq[None, :]
    cosine = jnp.cos(angles)[:, None, :]
    sine = jnp.sin(angles)[:, None, :]
    first_half = values[..., :half_size]
    second_half = values[..., half_size:]
    return jnp.concatenate(
        [first_half * cosine - second_half * sine, second_half * cosine + first_half * sine],
        axis=-1,
    )


def per_device(
    hidden_in,
    queries,
    fresh_key_value,
    positions,
    lengths,
    cache,
    out_proj,
    norm_gain,
    expert_ids,
    router_weights,
    gate_up,
    down,
):
    tp_count = lax.axis_size("tp")
    req_count = lax.axis_size("req")
    tp_index = lax.axis_index("tp")
    req_index = lax.axis_index("req")
    row_count = hidden_in.shape[0]
    head_size = cache.shape[3]
    kv_count = cache.shape[2]
    own_heads = queries.shape[1] // head_size
    head_count = own_heads * tp_count
    request_group_size = head_count // kv_count
    score_scaling = head_size ** (-0.5)
    model_width = norm_gain.shape[0]
    own_width = hidden_in.shape[1]
    first_head = tp_index * own_heads
    span_rows = cache.shape[0]
    q_local = apply_rotary_heads(
        queries.reshape(row_count, own_heads, head_size).astype(jnp.float32), positions, head_size
    ).astype(jnp.bfloat16)
    packed = jnp.stack([q_local.reshape(row_count, own_width), hidden_in], axis=0)
    gathered = lax.all_gather(packed, "tp", axis=0)
    q_all = jnp.transpose(gathered[:, 0], (1, 0, 2)).reshape(
        row_count, kv_count, request_group_size, head_size
    )
    hidden_full = jnp.transpose(gathered[:, 1], (1, 0, 2)).reshape(row_count, model_width)
    k_new = apply_rotary_heads(
        fresh_key_value[:, 0].reshape(row_count, kv_count, head_size).astype(jnp.float32),
        positions,
        head_size,
    ).astype(jnp.bfloat16)
    value_fresh = fresh_key_value[:, 1].reshape(row_count, kv_count, head_size)
    own_score = (
        jnp.einsum("rcgd,rcd->rcg", q_all, k_new, preferred_element_type=jnp.float32)
        * score_scaling
    )
    segment_ends = jnp.cumsum(lengths[0], dtype=jnp.int32)
    segment_starts = segment_ends - lengths[0]
    cache_spots = tp_index * span_rows + jnp.arange(span_rows, dtype=jnp.int32)
    mask = (cache_spots[None, :] >= segment_starts[:, None]) & (
        cache_spots[None, :] < segment_ends[:, None]
    )
    mask = mask[:, None, None, :]
    keys = cache[:, 0]
    values = cache[:, 1]
    scores = (
        jnp.einsum("rcgd,jcd->rcgj", q_all, keys, preferred_element_type=jnp.float32)
        * score_scaling
    )
    scores = jnp.where(mask, scores, neg_floor)
    highest_local = jnp.max(scores, axis=3)
    weights = jnp.where(mask, jnp.exp(scores - highest_local[..., None]), 0.0)
    totals_local = jnp.sum(weights, axis=3)
    sums_local = jnp.einsum(
        "rcgj,jcd->rcgd",
        weights,
        values.astype(jnp.float32),
        precision=lax.Precision.HIGHEST,
        preferred_element_type=jnp.float32,
    )
    states = jnp.concatenate(
        [highest_local[..., None], totals_local[..., None], sums_local], axis=3
    ).reshape(row_count, head_count, head_size + 2)
    all_states = lax.all_gather(states, "tp", axis=0)
    all_states = lax.dynamic_slice_in_dim(all_states, first_head, own_heads, 2)
    parts_highest = all_states[..., 0]
    parts_totals = all_states[..., 1]
    parts_sums = all_states[..., 2:]
    own_slice = lax.dynamic_slice_in_dim(
        own_score.reshape(row_count, head_count), first_head, own_heads, 1
    )
    top_score = jnp.maximum(jnp.max(parts_highest, axis=0), own_slice)
    factors = jnp.exp(parts_highest - top_score[None])
    own_part = jnp.exp(own_slice - top_score)
    head_kv = (first_head + jnp.arange(own_heads, dtype=jnp.int32)) // request_group_size
    own_values = jnp.take(value_fresh, head_kv, axis=1).astype(jnp.float32)
    totals = jnp.sum(parts_totals * factors, axis=0) + own_part
    summed = jnp.sum(parts_sums * factors[..., None], axis=0) + own_values * own_part[..., None]
    attention_output = (
        (summed / totals[..., None]).astype(jnp.bfloat16).reshape(row_count, own_heads * head_size)
    )
    partial_proj = jnp.dot(attention_output, out_proj, preferred_element_type=jnp.float32)
    projected = lax.psum(partial_proj, "tp")
    residual = hidden_full.astype(jnp.float32) + projected
    mean_square = jnp.mean(residual * residual, axis=1, keepdims=True)
    normed = (residual * lax.rsqrt(mean_square + norm_eps) * norm_gain[None, :]).astype(
        jnp.bfloat16
    )
    local_count = gate_up.shape[0]
    block_total = local_count * req_count
    split_count = max(1, block_total // EXPERTS)
    expert_range = jnp.arange(EXPERTS, dtype=jnp.int32)
    member = jnp.any(expert_ids[:, :, None] == expert_range[None, None, :], axis=1)
    member_int = member.astype(jnp.int32)
    slot_of = jnp.cumsum(member_int, axis=0, dtype=jnp.int32) - member_int
    slot_taken = jnp.take_along_axis(slot_of, expert_ids, axis=1)
    block_taken = slot_taken % split_count * EXPERTS + expert_ids
    block_range = jnp.arange(block_total, dtype=jnp.int32)
    block_weights = jnp.sum(
        jnp.where(
            block_taken[:, :, None] == block_range[None, None, :], router_weights[:, :, None], 0.0
        ),
        axis=1,
    )
    rows_all = lax.all_gather(normed, "req", axis=0, tiled=True)
    weights_all = lax.all_gather(block_weights, "req", axis=0, tiled=True)
    weights_own = lax.dynamic_slice_in_dim(weights_all, req_index * local_count, local_count, 1)
    mixed = jnp.zeros((rows_all.shape[0], model_width), jnp.float32)
    for local_block in range(local_count):
        gate_part = jnp.dot(rows_all, gate_up[local_block, 0], preferred_element_type=jnp.float32)
        up_part = jnp.dot(rows_all, gate_up[local_block, 1], preferred_element_type=jnp.float32)
        activation = (jnp.maximum(gate_part, 0.0) * up_part).astype(jnp.bfloat16)
        produced = jnp.dot(activation, down[local_block], preferred_element_type=jnp.float32)
        produced = produced.astype(jnp.bfloat16).astype(jnp.float32)
        mixed = mixed + weights_own[:, local_block : local_block + 1] * produced
    mixed = mixed.reshape(req_count, row_count, tp_count, own_width)
    mixed = jnp.transpose(mixed, (0, 2, 1, 3)).reshape(req_count * tp_count, row_count, own_width)
    mixed = lax.psum_scatter(mixed, ("req", "tp"), scatter_dimension=0, tiled=True)
    mixed = mixed.reshape(row_count, own_width)
    residual_own = lax.dynamic_slice_in_dim(residual, tp_index * own_width, own_width, 1)
    return (residual_own + mixed).astype(jnp.bfloat16)


def solution(mesh):
    placed = (
        P("req", "tp"),
        P("req", "tp"),
        P("req", None, None),
        P("req"),
        P("req", None),
        P(("req", "tp"), None, None, None),
        P("tp", None),
        P(),
        P("req", None),
        P("req", None),
        P("req", None, None, "tp"),
        P("req", "tp", None),
    )
    return jax.shard_map(
        per_device, mesh=mesh, in_specs=placed, out_specs=P("req", "tp"), check_vma=False
    )
```

profile of v0, /device:TPU:0, one launch (start us, length us, event | category | flops | bytes accessed | tf_op | source)
XLA Modules:
  0.0 226.4 jit_solution(6006693005743040945)
XLA Ops:
  6.6 0.8 convert_element_type.94
  7.4 0.7 reshape.253
  8.5 0.7 pad_maximum_fusion.1
  9.2 6.6 %all-gather = bf16[8,24,384]{2,1,0:T(8,128)(2,1)S(1)} all-gather(bf16[2,24,384]{2,1,0:T(8,128)(2,1)S(1)} %pad_maximum_fusion.1), channel_id=2, replica_groups=mesh['req'=8,'tp'=4] {'tp'}, dimensions={0}, use_global_device_ids=true | all-gather | bytes 184320 | tf_op jit(solution)/shard_map/all_gather | solution.py:60
  17.8 0.7 fusion.17
  18.9 11.1 %all_gather.17 = f32[4,24,12,130]{3,1,2,0:T(8,128)S(1)} all-gather(f32[1,24,12,130]{3,1,2,0:T(8,128)S(1)} %pad_maximum_fusion), channel_id=1, replica_groups=mesh['req'=8,'tp'=4] {'tp'}, dimensions={0}, use_global_device_ids=true | all-gather | bytes 748800 | tf_op jit(solution)/shard_map/all_gather | solution.py:102
  31.3 0.6 multiply_reduce_fusion
  33.3 0.9 fusion.60
  34.5 31.0 %all_gather.18 = f32[192,32]{1,0:T(8,128)S(1)} all-gather(f32[24,32]{1,0:T(8,128)S(1)} %select_reduce_fusion), channel_id=1, replica_groups=mesh['req'=8,'tp'=4] {'req'}, dimensions={0}, use_global_device_ids=true | all-gather | bytes 27648 | tf_op jit(solution)/shard_map/all_gather | solution.py:144
  65.8 1.0 all-reduce.3.cloned.1.call-done
  66.8 1.0 multiply_reduce_fusion.1
  68.0 31.8 %all_gather.19 = bf16[192,1536]{1,0:T(8,128)(2,1)S(1)} all-gather(bf16[24,1536]{1,0:T(8,128)(2,1)S(1)} %multiply_convert_fusion), channel_id=1, replica_groups=mesh['req'=8,'tp'=4] {'req'}, dimensions={0}, use_global_device_ids=true | all-gather | bytes 663552 | tf_op jit(solution)/shard_map/all_gather | solution.py:143
  99.8 2.1 convolution_maximum_fusion.3
  101.9 2.1 convolution_maximum_fusion.2
  104.0 1.4 convolution_maximum_fusion.1
  105.4 1.4 convolution_maximum_fusion
  106.8 2.2 fusion.10
  109.0 3.2 %fusion.8 = f32[192,1536]{1,0:T(8,128)} fusion(f32[192,1536]{1,0:T(8,128)S(1)} %fusion.10, f32[192,192]{1,0:T(8,128)} %convolution_maximum_fusion.2, bf16[192,1536]{1,0:T(8,128)(2,1)S(1)} %all_gather.19, bf16[4,192,1536]{2,1,0:T(8,128)(2,1)} %param.23, bf16[4,2,1536,192]{2,3,1,0:T(8,128)(2,1)} %param.22, f32[192]{0:T(256)S(1)} %get-tuple-element.7), kind=kOutput, calls=%fused_computation.12 | convolution fusion | flops 227745792 | bytes 4326144 | tf_op jit(solution)/shard_map/dot_general | solution.py:151
  112.2 2.5 %fusion.5 = f32[192,1536]{1,0:T(8,128)S(1)} fusion(f32[192,1536]{1,0:T(8,128)} %fusion.8, f32[192,192]{1,0:T(8,128)S(1)} %convolution_maximum_fusion.1, bf16[192,1536]{1,0:T(8,128)(2,1)S(1)} %all_gather.19, bf16[4,192,1536]{2,1,0:T(8,128)(2,1)} %param.23, bf16[4,2,1536,192]{2,3,1,0:T(8,128)(2,1)} %param.22, f32[192]{0:T(256)S(1)} %get-tuple-element.6), kind=kOutput, calls=%fused_computation.8 | convolution fusion | flops 227745792 | bytes 4276992 | tf_op jit(solution)/shard_map/dot_general | solution.py:151
  114.7 3.1 %fusion.2 = f32[192,1536]{1,0:T(8,128)} fusion(f32[192,1536]{1,0:T(8,128)S(1)} %fusion.5, f32[192,192]{1,0:T(8,128)S(1)} %convolution_maximum_fusion, bf16[192,1536]{1,0:T(8,128)(2,1)S(1)} %all_gather.19, bf16[4,192,1536]{2,1,0:T(8,128)(2,1)} %param.23, bf16[4,2,1536,192]{2,3,1,0:T(8,128)(2,1)} %param.22, f32[192]{0:T(256)S(1)} %get-tuple-element.5), kind=kOutput, calls=%fused_computation.4 | convolution fusion | flops 227745792 | bytes 4276992 | tf_op jit(solution)/shard_map/dot_general | solution.py:151
  117.8 1.7 reshape.250
  119.5 1.1 copy.71
  120.6 97.6 %reduce-scatter.4.cloned.1.call-done = f32[1,24,384]{2,1,0:T(8,128)} async-done(((f32[32,24,384]{2,1,0:T(8,128)}), f32[1,24,384]{2,1,0:T(8,128)}) %reduce-scatter.4.cloned.1.call-update) | async-done | bytes 36880
  218.2 1.4 fusion.57
  (71 shorter events, 5.9 us)
Async XLA Ops:
  6.5 26.7 %copy-start = (bf16[384,1536]{1,0:T(8,128)(2,1)S(1)}, bf16[384,1536]{1,0:T(8,128)(2,1)}, u32[]{:S(2)}) copy-start(bf16[384,1536]{1,0:T(8,128)(2,1)} %param.18) | copy-start | bytes 3538948
  6.5 9.4 %copy-start.6 = (s32[1,24]{1,0:T(1,128)S(1)}, s32[1,24]{1,0:T(1,128)}, u32[]{:S(2)}) copy-start(s32[1,24]{1,0:T(1,128)} %param.16) | copy-start | bytes 292
  6.5 9.7 %copy-start.1 = (bf16[768,2,2,128]{3,2,1,0:T(2,128)(2,1)S(1)}, bf16[768,2,2,128]{3,2,1,0:T(2,128)(2,1)}, u32[]{:S(2)}) copy-start(bf16[768,2,2,128]{3,2,1,0:T(2,128)(2,1)} %param.17) | copy-start | bytes 2359300
  6.5 60.3 %all-reduce.3.cloned.1.call-start = ((), (), s32[]{:S(2)}) async-start(), calls=%async_computation.1 | async-start | bytes 294912 | tf_op jit(solution)/shard_map/psum | solution.py:121
  18.5 11.4 %copy-start.2 = (bf16[24,2,256]{2,1,0:T(2,128)(2,1)S(1)}, bf16[24,2,256]{2,1,0:T(2,128)(2,1)}, u32[]{:S(2)}) copy-start(bf16[24,2,256]{2,1,0:T(2,128)(2,1)} %param.14) | copy-start | bytes 73732
  33.0 1.3 copy-start.4
  33.1 1.3 copy-start.5
  34.2 33.7 %copy-start.3 = (f32[1536]{0:T(1024)S(1)}, f32[1536]{0:T(1024)}, u32[]{:S(2)}) copy-start(f32[1536]{0:T(1024)} %param.19) | copy-start | bytes 18436
  34.2 184.0 %reduce-scatter.4.cloned.1.call-start = ((), (), s32[]{:S(2)}) async-start(), calls=%async_computation.2 | async-start | bytes 1216512
Sparse Core Ops, SparseCore 0:
  34.3 32.4 all-reduce.2
  120.7 97.4 reduce-scatter.3
where the time goes:
time: 227 us; the launch traced here: 226 us
  waiting for transfers between devices  98.7 us (43%)
  blocking collectives  80.5 us (35%)
  matrix products  20.2 us (9%)
  between operations  13.8 us (6%)
  local copies, waits for them, and re-layouts  6.85 us (3%)
  other arithmetic  6.41 us (3%)
    unnamed x3, waiting for transfers between devices  97.7 us
    all_gather x1, blocking collectives, per_device(): rows_all = lax.all_gather(normed, 'req', axis=0, tiled=True)  31.8 us
    all_gather x1, blocking collectives, per_device(): weights_all = lax.all_gather(block_weights, 'req', axis=0, tiled=True)  31 us
    all_gather x1, blocking collectives, per_device(): all_states = lax.all_gather(states, 'tp', axis=0)  11.1 us
    dot_general x4, matrix products, per_device(): jnp.dot(activation, down[local_block], preferred_element_type=jnp.float32)  11 us
    dot_general x4, matrix products, per_device(): jnp.dot(rows_all, gate_up[local_block, 0], preferred_element_type=jnp.flo...  6.93 us
    all_gather x1, blocking collectives, per_device(): gathered = lax.all_gather(packed, 'tp', axis=0)  6.58 us
  transfers between devices with their start and end apart: 2, of which 2 were waited for; matrix products, arithmetic and copies ran while one was open for 0% of the time, Pallas kernels for 0%

commit v1 on v0

--- a/solution.py
+++ b/solution.py
@@ -140,8 +140,11 @@
         ),
         axis=1,
     )
-    rows_all = lax.all_gather(normed, "req", axis=0, tiled=True)
-    weights_all = lax.all_gather(block_weights, "req", axis=0, tiled=True)
+    rows_all, weights_all = jnp.split(
+        lax.all_gather(jnp.concatenate([normed, block_weights], axis=1), "req", axis=0, tiled=True),
+        [normed.shape[1]],
+        axis=1,
+    )
     weights_own = lax.dynamic_slice_in_dim(weights_all, req_index * local_count, local_count, 1)
     mixed = jnp.zeros((rows_all.shape[0], model_width), jnp.float32)
     for local_block in range(local_count):

time: 227 us -> 240 us (1.057)
  waiting for transfers between devices: 98.7 us -> 171 us
  blocking collectives: 80.5 us -> 17.7 us
    all_gather x2 -> x0, blocking collectives: 62.8 us -> none  [the longest x1 31.8 us: per_device(): rows_all = lax.all_gather(normed, 'req', axis=0, tiled=True)]
    all_gather x0 -> x1, waiting for transfers between devices: none -> 42.7 us  [per_device(): lax.all_gather(jnp.concatenate([normed, block_weights], axis=1), 'req', a...]
    psum x1, waiting for transfers between devices: 1.03 us -> 32.4 us  [per_device(): projected = lax.psum(partial_proj, 'tp')]
    dot_general x4, matrix products: 11 us -> 13.6 us  [per_device(): jnp.dot(activation, down[local_block], preferred_element_type=jnp.float32)]
    unnamed x3 -> x4, waiting for transfers between devices: 97.7 us -> 96.1 us
  transfers between devices with their start and end apart: 2 -> 3, of which waited for: 2 -> 3; matrix products, arithmetic and copies ran while one was open for 0% -> 0% of each run, Pallas kernels for 0% -> 0%
where the time goes in v1:
time: 240 us; the launch traced here: 239 us
  waiting for transfers between devices  171 us (71%)
  matrix products  21.8 us (9%)
  blocking collectives  17.7 us (7%)
  between operations  13.5 us (6%)
  local copies, waits for them, and re-layouts  7.83 us (3%)
  other arithmetic  7.08 us (3%)
    unnamed x4, waiting for transfers between devices  96.1 us
    all_gather x1, waiting for transfers between devices, per_device(): lax.all_gather(jnp.concatenate([normed, block_weights], axis=1), 'req', a...  42.7 us
    psum x1, waiting for transfers between devices, per_device(): projected = lax.psum(partial_proj, 'tp')  32.4 us
    dot_general x4, matrix products, per_device(): jnp.dot(activation, down[local_block], preferred_element_type=jnp.float32)  13.6 us
    all_gather x1, blocking collectives, per_device(): all_states = lax.all_gather(states, 'tp', axis=0)  11.1 us
    all_gather x1, blocking collectives, per_device(): gathered = lax.all_gather(packed, 'tp', axis=0)  6.58 us
    dot_general x4, matrix products, per_device(): jnp.dot(rows_all, gate_up[local_block, 0], preferred_element_type=jnp.flo...  5.94 us
  transfers between devices with their start and end apart: 3, of which 3 were waited for; matrix products, arithmetic and copies ran while one was open for 0% of the time, Pallas kernels for 0%

profile of v1, /device:TPU:0, one launch (start us, length us, event | category | flops | bytes accessed | tf_op | source)
XLA Modules:
  0.0 239.1 jit_solution(13828126473498780723)
XLA Ops:
  6.6 0.8 convert_element_type.97
  7.4 0.7 reshape.253
  8.5 0.7 pad_maximum_fusion.2
  9.2 6.6 %all-gather = bf16[8,24,384]{2,1,0:T(8,128)(2,1)S(1)} all-gather(bf16[2,24,384]{2,1,0:T(8,128)(2,1)S(1)} %pad_maximum_fusion.2), channel_id=2, replica_groups=mesh['req'=8,'tp'=4] {'tp'}, dimensions={0}, use_global_device_ids=true | all-gather | bytes 184320 | tf_op jit(solution)/shard_map/all_gather | solution.py:60
  17.8 0.7 fusion.17
  18.9 11.1 %all_gather.14 = f32[4,24,12,130]{3,1,2,0:T(8,128)S(1)} all-gather(f32[1,24,12,130]{3,1,2,0:T(8,128)S(1)} %pad_maximum_fusion), channel_id=1, replica_groups=mesh['req'=8,'tp'=4] {'tp'}, dimensions={0}, use_global_device_ids=true | all-gather | bytes 748800 | tf_op jit(solution)/shard_map/all_gather | solution.py:102
  33.3 0.9 fusion.73
  34.4 32.4 %all-reduce.3.cloned.1.call-done = f32[24,1536]{1,0:T(8,128)} async-done(((f32[24,1536]{1,0:T(8,128)}), f32[24,1536]{1,0:T(8,128)}) %all-reduce.3.cloned.1.call-update) | async-done | bytes 147472 | tf_op jit(solution)/shard_map/psum | solution.py:121
  66.8 1.0 multiply_reduce_fusion.1
  68.0 0.7 pad_maximum_fusion.1
  68.7 42.7 %all-gather.3.cloned.1.call-done = f32[192,1568]{1,0:T(8,128)} async-done(((f32[24,1568]{1,0:T(8,128)}), f32[192,1568]{1,0:T(8,128)}) %all-gather.3.cloned.1.call-update) | async-done | bytes 1204240 | tf_op jit(solution)/shard_map/all_gather | solution.py:144
  111.5 1.0 split.8
  112.8 1.8 convolution_maximum_fusion.3
  114.6 1.4 convolution_maximum_fusion.2
  116.0 1.4 convolution_maximum_fusion.1
  117.4 1.4 convolution_maximum_fusion
  118.8 3.1 %fusion.10 = f32[192,1536]{1,0:T(8,128)} fusion(f32[192,192]{1,0:T(8,128)S(1)} %convolution_maximum_fusion.3, f32[192,1568]{1,0:T(8,128)S(1)} %copy-done.1, bf16[4,192,1536]{2,1,0:T(8,128)(2,1)} %param.23, bf16[4,2,1536,192]{2,3,1,0:T(8,128)(2,1)} %param.22, f32[192]{0:T(256)S(1)} %get-tuple-element.8), kind=kOutput, calls=%fused_computation.15 | convolution fusion | flops 227450880 | bytes 3146752 | tf_op jit(solution)/shard_map/dot_general | solution.py:154
  121.9 3.5 %fusion.8 = f32[192,1536]{1,0:T(8,128)} fusion(f32[192,1536]{1,0:T(8,128)} %fusion.10, f32[192,192]{1,0:T(8,128)S(1)} %convolution_maximum_fusion.2, f32[192,1568]{1,0:T(8,128)S(1)} %copy-done.1, bf16[4,192,1536]{2,1,0:T(8,128)(2,1)} %param.23, bf16[4,2,1536,192]{2,3,1,0:T(8,128)(2,1)} %param.22, f32[192]{0:T(256)S(1)} %get-tuple-element.7), kind=kOutput, calls=%fused_computation.12 | convolution fusion | flops 227745792 | bytes 4326400 | tf_op jit(solution)/shard_map/dot_general | solution.py:154
  125.4 3.5 %fusion.5 = f32[192,1536]{1,0:T(8,128)} fusion(f32[192,1536]{1,0:T(8,128)} %fusion.8, f32[192,192]{1,0:T(8,128)S(1)} %convolution_maximum_fusion.1, f32[192,1568]{1,0:T(8,128)S(1)} %copy-done.1, bf16[4,192,1536]{2,1,0:T(8,128)(2,1)} %param.23, bf16[4,2,1536,192]{2,3,1,0:T(8,128)(2,1)} %param.22, f32[192]{0:T(256)S(1)} %get-tuple-element.6), kind=kOutput, calls=%fused_computation.8 | convolution fusion | flops 227745792 | bytes 4326400 | tf_op jit(solution)/shard_map/dot_general | solution.py:154
  128.9 3.5 %fusion.2 = f32[192,1536]{1,0:T(8,128)} fusion(f32[192,1536]{1,0:T(8,128)} %fusion.5, f32[192,192]{1,0:T(8,128)S(1)} %convolution_maximum_fusion, f32[192,1568]{1,0:T(8,128)S(1)} %copy-done.1, bf16[4,192,1536]{2,1,0:T(8,128)(2,1)} %param.23, bf16[4,2,1536,192]{2,3,1,0:T(8,128)(2,1)} %param.22, f32[192]{0:T(256)S(1)} %get-tuple-element.5), kind=kOutput, calls=%fused_computation.4 | convolution fusion | flops 227745792 | bytes 4326400 | tf_op jit(solution)/shard_map/dot_general | solution.py:154
  132.4 1.7 reshape.250
  134.1 1.1 copy.71
  135.2 96.0 %reduce-scatter.4.cloned.1.call-done = f32[1,24,384]{2,1,0:T(8,128)} async-done(((f32[32,24,384]{2,1,0:T(8,128)}), f32[1,24,384]{2,1,0:T(8,128)}) %reduce-scatter.4.cloned.1.call-update) | async-done | bytes 36880
  231.2 1.4 fusion.70
  (76 shorter events, 6.6 us)
Async XLA Ops:
  6.5 26.7 %copy-start = (bf16[384,1536]{1,0:T(8,128)(2,1)S(1)}, bf16[384,1536]{1,0:T(8,128)(2,1)}, u32[]{:S(2)}) copy-start(bf16[384,1536]{1,0:T(8,128)(2,1)} %param.18) | copy-start | bytes 3538948
  6.5 9.4 %copy-start.7 = (s32[1,24]{1,0:T(1,128)S(1)}, s32[1,24]{1,0:T(1,128)}, u32[]{:S(2)}) copy-start(s32[1,24]{1,0:T(1,128)} %param.16) | copy-start | bytes 292
  6.5 9.7 %copy-start.2 = (bf16[768,2,2,128]{3,2,1,0:T(2,128)(2,1)S(1)}, bf16[768,2,2,128]{3,2,1,0:T(2,128)(2,1)}, u32[]{:S(2)}) copy-start(bf16[768,2,2,128]{3,2,1,0:T(2,128)(2,1)} %param.17) | copy-start | bytes 2359300
  6.5 60.3 %all-reduce.3.cloned.1.call-start = ((), (), s32[]{:S(2)}) async-start(), calls=%async_computation.1 | async-start | bytes 294912 | tf_op jit(solution)/shard_map/psum | solution.py:121
  18.5 11.4 %copy-start.3 = (bf16[24,2,256]{2,1,0:T(2,128)(2,1)S(1)}, bf16[24,2,256]{2,1,0:T(2,128)(2,1)}, u32[]{:S(2)}) copy-start(bf16[24,2,256]{2,1,0:T(2,128)(2,1)} %param.14) | copy-start | bytes 73732
  32.0 2.3 copy-start.5
  32.0 2.3 copy-start.6
  33.2 34.6 %copy-start.4 = (f32[1536]{0:T(1024)S(1)}, f32[1536]{0:T(1024)}, u32[]{:S(2)}) copy-start(f32[1536]{0:T(1024)} %param.19) | copy-start | bytes 18436
  34.2 77.2 %all-gather.3.cloned.1.call-start = ((), (), s32[]{:S(2)}) async-start(), calls=%async_computation.2 | async-start | bytes 1437696 | tf_op jit(solution)/shard_map/all_gather | solution.py:144
  68.7 162.5 %reduce-scatter.4.cloned.1.call-start = ((), (), s32[]{:S(2)}) async-start(), calls=%async_computation.3 | async-start | bytes 1216512
  111.5 3.1 %copy-start.1 = (f32[192,1568]{1,0:T(8,128)S(1)}, f32[192,1568]{1,0:T(8,128)}, u32[]{:S(2)}) copy-start(f32[192,1568]{1,0:T(8,128)} %all-gather.3.cloned.1.call-done) | copy-start | bytes 3612676
Sparse Core Ops, SparseCore 0:
  34.3 32.4 all-reduce.2
  69.0 42.4 all-gather.2
  135.3 95.8 reduce-scatter.3
